TPU v7x, 512 devices: a whole 4x8x8 slice. The times are simulated.
512 devices in a mesh: section: 32 (over z, x), et: 16 (over y, core).
Axes of the slice: x: 4, y: 8, z: 8, core: 2. Of those that a mesh axis runs over, the one named last changes fastest.
Arguments:
- x_fwd: bfloat16 [32, 256, 3072], P('section', 'et'), may hold values from -6 to 6
- act_fwd: bfloat16 [32, 256, 8192], P('section', None, 'et'), may hold values from -6 to 6
- ids_fwd: int32 [32, 256, 2], P('section'), may hold values from 0 to 7, as said below
- x_bwd: bfloat16 [32, 256, 3072], P('section', 'et'), may hold values from -6 to 6
- act_bwd: bfloat16 [32, 256, 8192], P('section', None, 'et'), may hold values from -6 to 6
- ids_bwd: int32 [32, 256, 2], P('section'), may hold values from 0 to 7, as said below
- grad_out: bfloat16 [32, 256, 3072], P('section', 'et'), may hold values from -6 to 6
- gain: bfloat16 [32, 3072], P('section'), may hold values from 0.099609375 to 1.8984375
- w_router: bfloat16 [32, 3072, 8], P('section'), may hold values from -0.21875 to 0.21875
- w_down: bfloat16 [32, 8192, 3072], P('section', 'et'), may hold values from -0.0625 to 0.0625
Outputs:
- fwd_in: bfloat16 [32, 256, 3072], P('section', 'et')
- incoming_gradient: bfloat16 [32, 256, 3072], P('section', 'et')
- dact: bfloat16 [32, 256, 8192], P('section', None, 'et')
Inputs may be any that keep to these rules, and one draw needn't show every extreme that they name: `ids_fwd`: each token names 2 different experts; in each section's micro-batch exactly 128 tokens name expert 0. `ids_bwd`: each token names 2 different experts; in each section's micro-batch exactly 128 tokens name expert 0.
All inputs are finite; a program needn't handle non-finite values.
Results may differ from a plain program's by a relative error of at most 0.014.
Values may be sent and summed in bfloat16 or wider, within the bound.
No kernel may reach another device: no remote copies, remote signals or barrier semaphores. Data moves between devices by JAX's collectives and lax.ppermute only.
A program may use at most 64 MiB of HBM per device.

v0:
```python
import jax
import jax.numpy as jnp
from jax import lax
from jax.sharding import PartitionSpec as P


def from_behind(value, axis, steps):
    count = lax.axis_size(axis)
    first, last = (max(0, -steps), min(count, count - steps))
    return lax.ppermute(value, axis, [(source, source + steps) for source in range(first, last)])


def norm_logits(inputs, gain, w_router):
    wide = inputs.astype(jnp.float32)
    inverse = lax.rsqrt(jnp.mean(wide * wide, axis=-1, keepdims=True) + 1e-05)
    normed = (wide * inverse * gain.astype(jnp.float32)).astype(jnp.bfloat16)
    logits = jnp.dot(normed, w_router, preferred_element_type=jnp.float32).astype(jnp.bfloat16)
    return (wide, inverse, logits)


def routing(logits, chosen, experts):
    route = jnp.sum((chosen == 0).astype(jnp.float32), axis=1)
    partner = jnp.minimum(jnp.sum(chosen, axis=1), experts - 1)
    labels = jnp.arange(experts, dtype=jnp.int32)
    onehot = (partner[:, None] == labels[None, :]).astype(jnp.float32)
    wide_logits = logits.astype(jnp.float32)
    sigma = jax.nn.sigmoid(wide_logits[:, 0] - jnp.sum(wide_logits * onehot, axis=1))
    return (route, onehot, sigma, route * sigma)


def arrange(chosen):
    member = jnp.sum((chosen == 0).astype(jnp.int32), axis=1)
    tally = jnp.sum(member)
    before = jnp.cumsum(member) - member
    after = jnp.cumsum(1 - member) - (1 - member)
    place = jnp.where(member == 1, before, tally + after)
    ordering = jnp.zeros_like(member).at[place].set(jnp.arange(member.shape[0], dtype=jnp.int32))
    return (member, place, ordering)


def spread_back(compact, member, place, capacity):
    safe = jnp.minimum(place, capacity - 1)
    return jnp.where(member[:, None] == 1, compact[safe], 0.0)


def shards(x_fwd, act_fwd, ids_fwd, x_bwd, act_bwd, ids_bwd, grad_out, gain, w_router, w_down):
    x_fwd, act_fwd, ids_fwd, x_bwd, act_bwd = (
        x_fwd[0],
        act_fwd[0],
        ids_fwd[0],
        x_bwd[0],
        act_bwd[0],
    )
    ids_bwd, grad_out, gain, w_router, w_down = (
        ids_bwd[0],
        grad_out[0],
        gain[0],
        w_router[0],
        w_down[0],
    )
    experts = w_router.shape[1]
    tokens = ids_fwd.shape[0]
    capacity = tokens // 2
    own_rows = x_fwd.shape[0]
    first_row = lax.axis_index("et") * own_rows
    wide_f, inverse_f, logit_f = norm_logits(x_fwd, gain, w_router)
    backward_wide_rows, backward_inverse_norm, logit_b = norm_logits(x_bwd, gain, w_router)
    full_f, full_b, full_g = (
        lax.all_gather(logit_f, "et", axis=0, tiled=True),
        lax.all_gather(logit_b, "et", axis=0, tiled=True),
        lax.all_gather(grad_out, "et", axis=0, tiled=True),
    )
    route_f, onehot_f, sigma_f, coef_f = routing(full_f, ids_fwd, experts)
    member_f, place_f, order_f = arrange(ids_fwd)
    chosen_f = order_f[:capacity]
    compact = (
        jnp.dot(act_fwd[chosen_f], w_down, preferred_element_type=jnp.float32)
        * coef_f[chosen_f][:, None]
    )
    summed = lax.psum(compact.astype(jnp.bfloat16), "et").astype(jnp.float32)
    member_own = lax.dynamic_slice_in_dim(member_f, first_row, own_rows, 0)
    place_own = lax.dynamic_slice_in_dim(place_f, first_row, own_rows, 0)
    y_mine = spread_back(summed, member_own, place_own, capacity)
    layer_out = (wide_f + y_mine).astype(jnp.bfloat16)
    route_b, onehot_b, sigma_b, backward_coefficient = routing(full_b, ids_bwd, experts)
    member_b, place_b, order_b = arrange(ids_bwd)
    chosen_b = order_b[:capacity]
    up_compact = lax.dot_general(
        full_g[chosen_b], w_down, (((1,), (1,)), ((), ())), preferred_element_type=jnp.float32
    )
    back_up = spread_back(up_compact, member_b, place_b, capacity)
    dact = (backward_coefficient[:, None] * back_up).astype(jnp.bfloat16)
    dprob_part = jnp.sum(act_bwd.astype(jnp.float32) * back_up, axis=1)
    dprob_all = lax.psum(dprob_part, "et")
    dprob_mine = lax.dynamic_slice_in_dim(dprob_all, first_row, own_rows, 0)
    route_mine = lax.dynamic_slice_in_dim(route_b, first_row, own_rows, 0)
    sigma_mine = lax.dynamic_slice_in_dim(sigma_b, first_row, own_rows, 0)
    onehot_mine = lax.dynamic_slice_in_dim(onehot_b, first_row, own_rows, 0)
    slope = route_mine * dprob_mine * sigma_mine * (1.0 - sigma_mine)
    router_wide = w_router.astype(jnp.float32)
    spread = router_wide[:, 0][None, :] - jnp.dot(
        onehot_mine, router_wide.T, precision=lax.Precision.HIGHEST
    )
    dnormed = slope[:, None] * spread
    scaled_rows = dnormed * gain.astype(jnp.float32)
    normalized_input = backward_wide_rows * backward_inverse_norm
    norm_input_gradient = backward_inverse_norm * (
        scaled_rows
        - normalized_input * jnp.mean(scaled_rows * normalized_input, axis=-1, keepdims=True)
    )
    input_grad = (grad_out.astype(jnp.float32) + norm_input_gradient).astype(jnp.bfloat16)
    fwd_in = from_behind(layer_out, "section", 1)
    incoming_gradient = from_behind(input_grad, "section", -1)
    return (fwd_in[None], incoming_gradient[None], dact[None])


def solution(mesh):
    placed = (
        P("section", "et", None),
        P("section", None, "et"),
        P("section", None, None),
        P("section", "et", None),
        P("section", None, "et"),
        P("section", None, None),
        P("section", "et", None),
        P("section", None),
        P("section", None, None),
        P("section", "et", None),
    )
    return jax.shard_map(
        shards,
        mesh=mesh,
        in_specs=placed,
        out_specs=(P("section", "et", None), P("section", "et", None), P("section", None, "et")),
        check_vma=False,
    )
```

profile of v0, /device:TPU:6, one launch (start us, length us, event | category | flops | bytes accessed | tf_op | source)
XLA Modules:
  0.0 256.7 jit_solution(1746351903962819599)
XLA Ops:
  8.1 1.4 convert_reduce_fusion
  11.9 1.4 scatter_custom_fusion
  16.3 17.6 %all-gather.1 = bf16[16,16,8]{1,2,0:T(8,128)(2,1)S(1)} all-gather(bf16[1,16,8]{1,2,0:T(8,128)(2,1)S(1)} %fusion.6), channel_id=1, replica_groups=mesh['section'=32,'et'=16] {'et'}, dimensions={0}, use_global_device_ids=true | all-gather | bytes 4352 | tf_op jit(solution)/shard_map/all_gather | solution.py:69
  34.1 1.9 gather_fusion
  36.0 1.3 gather_fusion.1
  37.3 1.5 fusion
  43.8 1.4 scatter_custom_fusion.1
  45.9 15.0 %all-gather.2 = bf16[16,16,8]{1,2,0:T(8,128)(2,1)S(1)} all-gather(bf16[1,16,8]{1,2,0:T(8,128)(2,1)S(1)} %fusion.7), channel_id=1, replica_groups=mesh['section'=32,'et'=16] {'et'}, dimensions={0}, use_global_device_ids=true | all-gather | bytes 4352 | tf_op jit(solution)/shard_map/all_gather | solution.py:70
  63.9 1.4 slice_convert_fusion
  65.3 92.2 %all-reduce.2.cloned.1.call-done = bf16[128,3072]{1,0:T(8,128)(2,1)} async-done(((bf16[128,3072]{1,0:T(8,128)(2,1)}), bf16[128,3072]{1,0:T(8,128)(2,1)}) %all-reduce.2.cloned.1.call-update) | async-done | bytes 786448 | tf_op jit(solution)/shard_map/psum | solution.py:80
  157.6 2.4 convert_element_type.106
  160.0 2.2 gather_fusion.2
  163.0 3.5 %collective-permute-start = (bf16[16,3072]{1,0:T(8,128)(2,1)S(1)}, bf16[16,3072]{1,0:T(8,128)(2,1)}, u32[]{:S(2)}, u32[]{:S(2)}) collective-permute-start(bf16[16,3072]{1,0:T(8,128)(2,1)S(1)} %fusion.23), channel_id=1, source_target_pairs={{0,16},{16,32},{32,48},{48,64},{64,80},{80,96},{96,112},{112,128},... | collective-permute-start | bytes 294920 | tf_op jit(solution)/shard_map/ppermute | solution.py:10
  167.2 2.4 collective-permute-done
  169.6 32.3 %all-gather.5.cloned.1.call-done = bf16[1,256,3072]{2,1,0:T(8,128)(2,1)} async-done(((bf16[1,16,3072]{2,1,0:T(8,128)(2,1)}), bf16[1,256,3072]{2,1,0:T(8,128)(2,1)}) %all-gather.5.cloned.1.call-update) | async-done | bytes 1572880 | tf_op jit(solution)/shard_map/all_gather | solution.py:71
  201.9 4.5 %gather_fusion.3 = bf16[128,3072]{1,0:T(8,128)(2,1)} fusion(bf16[256,3072]{1,0:T(8,128)(2,1)} %bitcast.108, s32[1024]{0:T(1024)} %pad_clamp_fusion.1), kind=kCustom, calls=%fused_computation.3 | custom fusion | bytes 1573376 | tf_op jit(solution)/shard_map/gather | solution.py:89
  206.3 2.3 fusion.3
  208.7 1.8 gather_fusion.4
  210.5 1.3 fusion.8
  211.8 24.9 %psum.15 = f32[256]{0:T(256)S(1)} all-reduce(f32[256]{0:T(256)S(1)} %fusion.8), channel_id=1, replica_groups=mesh['section'=32,'et'=16] {'et'}, use_global_device_ids=true, to_apply=%region_22.23 | all-reduce | flops 256 | bytes 2048 | tf_op jit(solution)/shard_map/psum | solution.py:94
  239.0 2.8 %collective-permute-start.1 = (bf16[16,3072]{1,0:T(8,128)(2,1)S(1)}, bf16[16,3072]{1,0:T(8,128)(2,1)S(1)}, u32[]{:S(2)}, u32[]{:S(2)}) collective-permute-start(bf16[16,3072]{1,0:T(8,128)(2,1)S(1)} %fusion.21), channel_id=1, source_target_pairs={{16,0},{32,16},{48,32},{64,48},{80,64},{96,80},{112,96},{128,112},... | collective-permute-start | bytes 294920 | tf_op jit(solution)/shard_map/ppermute | solution.py:10
  241.8 1.9 fusion.10
  243.7 4.0 %collective-permute-done.1 = bf16[16,3072]{1,0:T(8,128)(2,1)S(1)} collective-permute-done((bf16[16,3072]{1,0:T(8,128)(2,1)S(1)}, bf16[16,3072]{1,0:T(8,128)(2,1)S(1)}, u32[]{:S(2)}, u32[]{:S(2)}) %collective-permute-start.1) | collective-permute-done | bytes 98336 | tf_op jit(solution)/shard_map/ppermute | solution.py:10
  247.6 1.5 copy.20
  (87 shorter events, 19.5 us)
Async XLA Ops:
  7.2 30.1 %copy-start = (bf16[1,512,3072]{2,1,0:T(8,128)(2,1)S(1)}, bf16[1,512,3072]{2,1,0:T(8,128)(2,1)}, u32[]{:S(2)}) copy-start(bf16[1,512,3072]{2,1,0:T(8,128)(2,1)} %param.19) | copy-start | bytes 9437188
  7.2 150.4 %all-reduce.2.cloned.1.call-start = ((), (), s32[]{:S(2)}) async-start(), calls=%async_computation | async-start | bytes 1572864 | tf_op jit(solution)/shard_map/psum | solution.py:80
  34.0 6.2 %copy-start.2 = (bf16[1,16,3072]{2,1,0:T(8,128)(2,1)S(1)}, bf16[1,16,3072]{2,1,0:T(8,128)(2,1)}, u32[]{:S(2)}) copy-start(bf16[1,16,3072]{2,1,0:T(8,128)(2,1)} %param.13) | copy-start | bytes 294916
  35.9 25.7 %copy-start.4 = (s32[1,256,2]{1,2,0:T(2,128)S(1)}, s32[1,256,2]{1,2,0:T(2,128)}, u32[]{:S(2)}) copy-start(s32[1,256,2]{1,2,0:T(2,128)} %param.15) | copy-start | bytes 6148
  38.8 123.5 %copy-start.1 = (bf16[1,16,3072]{2,1,0:T(8,128)(2,1)S(1)}, bf16[1,16,3072]{2,1,0:T(8,128)(2,1)}, u32[]{:S(2)}) copy-start(bf16[1,16,3072]{2,1,0:T(8,128)(2,1)} %param.10) | copy-start | bytes 294916
  38.8 163.1 %all-gather.5.cloned.1.call-start = ((), (), s32[]{:S(2)}) async-start(), calls=%async_computation.1 | async-start | bytes 1671168 | tf_op jit(solution)/shard_map/all_gather | solution.py:71
  40.4 1.0 copy-start.9
  163.0 6.6 %collective-permute-start = (bf16[16,3072]{1,0:T(8,128)(2,1)S(1)}, bf16[16,3072]{1,0:T(8,128)(2,1)}, u32[]{:S(2)}, u32[]{:S(2)}) collective-permute-start(bf16[16,3072]{1,0:T(8,128)(2,1)S(1)} %fusion.23), channel_id=1, source_target_pairs={{0,16},{16,32},{32,48},{48,64},{64,80},{80,96},{96,112},{112,128},... | collective-permute-start | bytes 294920 | tf_op jit(solution)/shard_map/ppermute | solution.py:10
  208.7 1.8 copy-start.8
  208.7 28.0 %copy-start.6 = (f32[256]{0:T(256)S(1)}, f32[256]{0:T(256)}, u32[]{:S(2)}) copy-start(f32[256]{0:T(256)} %add_divide_fusion) | copy-start | bytes 3076
  208.7 28.1 %copy-start.3 = (f32[3072,1]{0,1:T(1,128)S(1)}, f32[3072,1]{0,1:T(1,128)}, u32[]{:S(2)}) copy-start(f32[3072,1]{0,1:T(1,128)} %slice_convert_fusion) | copy-start | bytes 36868
  208.7 28.1 %copy-start.7 = (pred[256,8]{0,1:T(8,128)(4,1)S(1)}, pred[256,8]{0,1:T(8,128)(4,1)}, u32[]{:S(2)}) copy-start(pred[256,8]{0,1:T(8,128)(4,1)} %iota_compare_fusion) | copy-start | bytes 6148
  208.7 33.1 %copy-start.5 = (f32[256,1]{0,1:T(1,128)S(1)}, f32[256,1]{0,1:T(1,128)}, u32[]{:S(2)}) copy-start(f32[256,1]{0,1:T(1,128)} %get-tuple-element.14) | copy-start | bytes 3076
  239.0 8.6 %collective-permute-start.1 = (bf16[16,3072]{1,0:T(8,128)(2,1)S(1)}, bf16[16,3072]{1,0:T(8,128)(2,1)S(1)}, u32[]{:S(2)}, u32[]{:S(2)}) collective-permute-start(bf16[16,3072]{1,0:T(8,128)(2,1)S(1)} %fusion.21), channel_id=1, source_target_pairs={{16,0},{32,16},{48,32},{64,48},{80,64},{96,80},{112,96},{128,112},... | collective-permute-start | bytes 294920 | tf_op jit(solution)/shard_map/ppermute | solution.py:10
Sparse Core Ops, SparseCore 0:
  38.9 118.5 all-reduce.1
  159.7 42.1 all-gather.4
where the time goes:
time: 257 us
  waiting for transfers between devices  132 us (51%)
  blocking collectives  57.5 us (22%)
  other arithmetic  22.1 us (9%)
  local copies, waits for them, and re-layouts  17.6 us (7%)
  between operations  14.3 us (6%)
  matrix products  7.15 us (3%)
  starting transfers between devices  6.38 us (2%)
    psum x1, waiting for transfers between devices, shards(): summed = lax.psum(compact.astype(jnp.bfloat16), 'et').astype(jnp.float32)  92.2 us
    all_gather x1, waiting for transfers between devices, shards(): lax.all_gather(grad_out, 'et', axis=0, tiled=True)  32.3 us
    psum x1, blocking collectives, shards(): dprob_all = lax.psum(dprob_part, 'et')  24.9 us
    all_gather x1, blocking collectives, shards(): lax.all_gather(logit_f, 'et', axis=0, tiled=True)  17.6 us
    all_gather x1, blocking collectives, shards(): lax.all_gather(logit_b, 'et', axis=0, tiled=True)  15 us
    ppermute x2, waiting for transfers between devices, from_behind(): lax.ppermute(value, axis, [(source, source + steps) for source in range(f...  6.38 us
    ppermute x2, starting transfers between devices, from_behind(): lax.ppermute(value, axis, [(source, source + steps) for source in range(f...  6.3 us
  transfers between devices with their start and end apart: 4, of which 4 were waited for; matrix products, arithmetic and copies ran while one was open for 7% of the time, Pallas kernels for 0%

commit v1 on v0

--- a/solution.py
+++ b/solution.py
@@ -2,6 +2,19 @@
 import jax.numpy as jnp
 from jax import lax
 from jax.sharding import PartitionSpec as P
+
+
+def ring_gather(shard, axis, dim):
+    ways = lax.axis_size(axis)
+    up = [(d, (d + 1) % ways) for d in range(ways)]
+    down = [(d, (d - 1) % ways) for d in range(ways)]
+    earlier, later = ([shard], [shard])
+    for _ in range(ways // 2):
+        earlier.append(lax.ppermute(earlier[-1], axis, up))
+    for _ in range((ways - 1) // 2):
+        later.append(lax.ppermute(later[-1], axis, down))
+    line = jnp.concatenate([*earlier[::-1], *later[1:]], axis=dim)
+    return jnp.roll(line, (lax.axis_index(axis) - ways // 2) * shard.shape[dim], axis=dim)
 
 
 def from_behind(value, axis, steps):
@@ -67,7 +80,7 @@
     backward_wide_rows, backward_inverse_norm, logit_b = norm_logits(x_bwd, gain, w_router)
     full_f, full_b, full_g = (
         lax.all_gather(logit_f, "et", axis=0, tiled=True),
-        lax.all_gather(logit_b, "et", axis=0, tiled=True),
+        ring_gather(logit_b, "et", 0),
         lax.all_gather(grad_out, "et", axis=0, tiled=True),
     )
     route_f, onehot_f, sigma_f, coef_f = routing(full_f, ids_fwd, experts)

time: 257 us -> 258 us (level)
  starting transfers between devices: 6.38 us -> 26.9 us
  blocking collectives: 57.5 us -> 42.6 us
  waiting for transfers between devices: 132 us -> 126 us
    ppermute x0 -> x15, starting transfers between devices: none -> 20.5 us  [the longest x7 20.1 us: ring_gather(): later.append(lax.ppermute(later[-1], axis, down))]
    psum x1, waiting for transfers between devices: 92.2 us -> 76.4 us  [shards(): summed = lax.psum(compact.astype(jnp.bfloat16), 'et').astype(jnp.float32)]
    all_gather x1 -> x0, blocking collectives: 15 us -> none  [shards(): lax.all_gather(logit_b, 'et', axis=0, tiled=True)]
    ppermute x0 -> x15, waiting for transfers between devices: none -> 11.4 us  [the longest x8 7.29 us: ring_gather(): earlier.append(lax.ppermute(earlier[-1], axis, up))]
  transfers between devices with their start and end apart: 4 -> 19, of which waited for: 4 -> 17; matrix products, arithmetic and copies ran while one was open for 7% -> 7% of each run, Pallas kernels for 0% -> 0%
where the time goes in v1:
time: 258 us; the launch traced here: 257 us
  waiting for transfers between devices  126 us (49%)
  blocking collectives  42.6 us (17%)
  starting transfers between devices  26.9 us (10%)
  other arithmetic  21.7 us (8%)
  local copies, waits for them, and re-layouts  17.7 us (7%)
  between operations  14.4 us (6%)
  matrix products  7.15 us (3%)
    psum x1, waiting for transfers between devices, shards(): summed = lax.psum(compact.astype(jnp.bfloat16), 'et').astype(jnp.float32)  76.4 us
    all_gather x1, waiting for transfers between devices, shards(): lax.all_gather(grad_out, 'et', axis=0, tiled=True)  32.3 us
    psum x1, blocking collectives, shards(): dprob_all = lax.psum(dprob_part, 'et')  24.9 us
    ppermute x7, starting transfers between devices, ring_gather(): later.append(lax.ppermute(later[-1], axis, down))  20.1 us
    all_gather x1, blocking collectives, shards(): lax.all_gather(logit_f, 'et', axis=0, tiled=True)  17.6 us
    ppermute x8, waiting for transfers between devices, ring_gather(): earlier.append(lax.ppermute(earlier[-1], axis, up))  7.29 us
    ppermute x2, waiting for transfers between devices, from_behind(): lax.ppermute(value, axis, [(source, source + steps) for source in range(f...  6.39 us
    ppermute x2, starting transfers between devices, from_behind(): lax.ppermute(value, axis, [(source, source + steps) for source in range(f...  6.3 us
  transfers between devices with their start and end apart: 19, of which 17 were waited for; matrix products, arithmetic and copies ran while one was open for 7% of the time, Pallas kernels for 0%

profile of v1, /device:TPU:6, one launch (start us, length us, event | category | flops | bytes accessed | tf_op | source)
XLA Modules:
  0.0 256.8 jit_solution(5038064221802888046)
XLA Ops:
  16.3 17.6 %all-gather.1 = bf16[16,16,8]{1,2,0:T(8,128)(2,1)S(1)} all-gather(bf16[1,16,8]{1,2,0:T(8,128)(2,1)S(1)} %fusion.6), channel_id=1, replica_groups=mesh['section'=32,'et'=16] {'et'}, dimensions={0}, use_global_device_ids=true | all-gather | bytes 4352 | tf_op jit(solution)/shard_map/all_gather | solution.py:82
  34.1 1.9 gather_fusion
  40.4 2.6 %collective-permute-start.9 = (bf16[16,8]{0,1:T(8,128)(2,1)S(1)}, bf16[16,8]{0,1:T(8,128)(2,1)S(1)}, u32[]{:S(2)}, u32[]{:S(2)}) collective-permute-start(bf16[16,8]{0,1:T(8,128)(2,1)S(1)} %convolution_convert_fusion), channel_id=1, source_target_pairs={{0,15},{1,0},{2,1},{3,2},{4,3},{5,4},{6,5},{7,6},{8,7},{9,8},{10,9... | collective-permute-start | bytes 776 | tf_op jit(solution)/shard_map/ppermute | solution.py:15
  51.4 3.0 %collective-permute-start.10 = (bf16[16,8]{0,1:T(8,128)(2,1)S(1)}, bf16[16,8]{0,1:T(8,128)(2,1)S(1)}, u32[]{:S(2)}, u32[]{:S(2)}) collective-permute-start(bf16[16,8]{0,1:T(8,128)(2,1)S(1)} %collective-permute-done.9), channel_id=1, source_target_pairs={{0,15},{1,0},{2,1},{3,2},{4,3},{5,4},{6,5},{7,6},{8,7},{9,8},{10,9... | collective-permute-start | bytes 776 | tf_op jit(solution)/shard_map/ppermute | solution.py:15
  55.7 2.9 %collective-permute-start.11 = (bf16[16,8]{0,1:T(8,128)(2,1)S(1)}, bf16[16,8]{0,1:T(8,128)(2,1)S(1)}, u32[]{:S(2)}, u32[]{:S(2)}) collective-permute-start(bf16[16,8]{0,1:T(8,128)(2,1)S(1)} %collective-permute-done.10), channel_id=1, source_target_pairs={{0,15},{1,0},{2,1},{3,2},{4,3},{5,4},{6,5},{7,6},{8,7},{9,8},{10,9... | collective-permute-start | bytes 776 | tf_op jit(solution)/shard_map/ppermute | solution.py:15
  59.9 2.9 %collective-permute-start.12 = (bf16[16,8]{0,1:T(8,128)(2,1)S(1)}, bf16[16,8]{0,1:T(8,128)(2,1)S(1)}, u32[]{:S(2)}, u32[]{:S(2)}) collective-permute-start(bf16[16,8]{0,1:T(8,128)(2,1)S(1)} %collective-permute-done.11), channel_id=1, source_target_pairs={{0,15},{1,0},{2,1},{3,2},{4,3},{5,4},{6,5},{7,6},{8,7},{9,8},{10,9... | collective-permute-start | bytes 776 | tf_op jit(solution)/shard_map/ppermute | solution.py:15
  64.1 2.9 %collective-permute-start.13 = (bf16[16,8]{0,1:T(8,128)(2,1)S(1)}, bf16[16,8]{0,1:T(8,128)(2,1)S(1)}, u32[]{:S(2)}, u32[]{:S(2)}) collective-permute-start(bf16[16,8]{0,1:T(8,128)(2,1)S(1)} %collective-permute-done.12), channel_id=1, source_target_pairs={{0,15},{1,0},{2,1},{3,2},{4,3},{5,4},{6,5},{7,6},{8,7},{9,8},{10,9... | collective-permute-start | bytes 776 | tf_op jit(solution)/shard_map/ppermute | solution.py:15
  68.4 2.9 %collective-permute-start.14 = (bf16[16,8]{0,1:T(8,128)(2,1)S(1)}, bf16[16,8]{0,1:T(8,128)(2,1)S(1)}, u32[]{:S(2)}, u32[]{:S(2)}) collective-permute-start(bf16[16,8]{0,1:T(8,128)(2,1)S(1)} %collective-permute-done.13), channel_id=1, source_target_pairs={{0,15},{1,0},{2,1},{3,2},{4,3},{5,4},{6,5},{7,6},{8,7},{9,8},{10,9... | collective-permute-start | bytes 776 | tf_op jit(solution)/shard_map/ppermute | solution.py:15
  72.6 2.9 %collective-permute-start.15 = (bf16[16,8]{0,1:T(8,128)(2,1)S(1)}, bf16[16,8]{0,1:T(8,128)(2,1)S(1)}, u32[]{:S(2)}, u32[]{:S(2)}) collective-permute-start(bf16[16,8]{0,1:T(8,128)(2,1)S(1)} %collective-permute-done.14), channel_id=1, source_target_pairs={{0,15},{1,0},{2,1},{3,2},{4,3},{5,4},{6,5},{7,6},{8,7},{9,8},{10,9... | collective-permute-start | bytes 776 | tf_op jit(solution)/shard_map/ppermute | solution.py:15
  76.8 3.5 %collective-permute-done.8 = bf16[16,8]{0,1:T(8,128)(2,1)S(1)} collective-permute-done((bf16[16,8]{0,1:T(8,128)(2,1)S(1)}, bf16[16,8]{0,1:T(8,128)(2,1)S(1)}, u32[]{:S(2)}, u32[]{:S(2)}) %collective-permute-start.8) | collective-permute-done | bytes 288 | tf_op jit(solution)/shard_map/ppermute | solution.py:13
  81.2 76.4 %all-reduce.2.cloned.1.call-done = bf16[128,3072]{1,0:T(8,128)(2,1)} async-done(((bf16[128,3072]{1,0:T(8,128)(2,1)}), bf16[128,3072]{1,0:T(8,128)(2,1)}) %all-reduce.2.cloned.1.call-update) | async-done | bytes 786448 | tf_op jit(solution)/shard_map/psum | solution.py:93
  157.6 2.4 convert_element_type.106
  160.0 2.2 gather_fusion.2
  163.0 3.5 %collective-permute-start = (bf16[16,3072]{1,0:T(8,128)(2,1)S(1)}, bf16[16,3072]{1,0:T(8,128)(2,1)}, u32[]{:S(2)}, u32[]{:S(2)}) collective-permute-start(bf16[16,3072]{1,0:T(8,128)(2,1)S(1)} %fusion.22), channel_id=1, source_target_pairs={{0,16},{16,32},{32,48},{48,64},{64,80},{80,96},{96,112},{112,128},... | collective-permute-start | bytes 294920 | tf_op jit(solution)/shard_map/ppermute | solution.py:23
  167.2 2.4 collective-permute-done
  169.6 32.3 %all-gather.4.cloned.1.call-done = bf16[1,256,3072]{2,1,0:T(8,128)(2,1)} async-done(((bf16[1,16,3072]{2,1,0:T(8,128)(2,1)}), bf16[1,256,3072]{2,1,0:T(8,128)(2,1)}) %all-gather.4.cloned.1.call-update) | async-done | bytes 1572880 | tf_op jit(solution)/shard_map/all_gather | solution.py:84
  201.9 4.5 %gather_fusion.3 = bf16[128,3072]{1,0:T(8,128)(2,1)} fusion(bf16[256,3072]{1,0:T(8,128)(2,1)} %bitcast.104, s32[1024]{0:T(1024)} %pad_clamp_fusion.1), kind=kCustom, calls=%fused_computation.3 | custom fusion | bytes 1573376 | tf_op jit(solution)/shard_map/gather | solution.py:102
  206.3 2.3 fusion.3
  208.7 1.9 gather_fusion.4
  211.9 24.9 %psum.15 = f32[256]{0:T(256)S(1)} all-reduce(f32[256]{0:T(256)S(1)} %fusion.7), channel_id=1, replica_groups=mesh['section'=32,'et'=16] {'et'}, use_global_device_ids=true, to_apply=%region_22.23 | all-reduce | flops 256 | bytes 2048 | tf_op jit(solution)/shard_map/psum | solution.py:107
  239.2 2.8 %collective-permute-start.16 = (bf16[16,3072]{1,0:T(8,128)(2,1)S(1)}, bf16[16,3072]{1,0:T(8,128)(2,1)S(1)}, u32[]{:S(2)}, u32[]{:S(2)}) collective-permute-start(bf16[16,3072]{1,0:T(8,128)(2,1)S(1)} %fusion.20), channel_id=1, source_target_pairs={{16,0},{32,16},{48,32},{64,48},{80,64},{96,80},{112,96},{128,112},... | collective-permute-start | bytes 294920 | tf_op jit(solution)/shard_map/ppermute | solution.py:23
  241.9 1.9 fusion.9
  243.8 4.0 %collective-permute-done.16 = bf16[16,3072]{1,0:T(8,128)(2,1)S(1)} collective-permute-done((bf16[16,3072]{1,0:T(8,128)(2,1)S(1)}, bf16[16,3072]{1,0:T(8,128)(2,1)S(1)}, u32[]{:S(2)}, u32[]{:S(2)}) %collective-permute-start.16) | collective-permute-done | bytes 98336 | tf_op jit(solution)/shard_map/ppermute | solution.py:23
  247.8 1.5 copy.19
  (118 shorter events, 36.3 us)
Async XLA Ops:
  7.2 30.1 %copy-start = (bf16[1,512,3072]{2,1,0:T(8,128)(2,1)S(1)}, bf16[1,512,3072]{2,1,0:T(8,128)(2,1)}, u32[]{:S(2)}) copy-start(bf16[1,512,3072]{2,1,0:T(8,128)(2,1)} %param.19) | copy-start | bytes 9437188
  7.2 150.4 %all-reduce.2.cloned.1.call-start = ((), (), s32[]{:S(2)}) async-start(), calls=%async_computation | async-start | bytes 1572864 | tf_op jit(solution)/shard_map/psum | solution.py:93
  38.8 123.5 %copy-start.1 = (bf16[1,16,3072]{2,1,0:T(8,128)(2,1)S(1)}, bf16[1,16,3072]{2,1,0:T(8,128)(2,1)}, u32[]{:S(2)}) copy-start(bf16[1,16,3072]{2,1,0:T(8,128)(2,1)} %param.10) | copy-start | bytes 294916
  38.8 163.1 %all-gather.4.cloned.1.call-start = ((), (), s32[]{:S(2)}) async-start(), calls=%async_computation.1 | async-start | bytes 1671168 | tf_op jit(solution)/shard_map/all_gather | solution.py:84
  40.0 10.8 %collective-permute-start.1 = (bf16[16,8]{0,1:T(8,128)(2,1)S(1)}, bf16[16,8]{0,1:T(8,128)(2,1)S(1)}, u32[]{:S(2)}, u32[]{:S(2)}) collective-permute-start(bf16[16,8]{0,1:T(8,128)(2,1)S(1)} %convolution_convert_fusion), channel_id=1, source_target_pairs={{0,1},{1,2},{2,3},{3,4},{4,5},{5,6},{6,7},{7,8},{8,9},{9,10},{10,1... | collective-permute-start | bytes 776 | tf_op jit(solution)/shard_map/ppermute | solution.py:13
  40.4 11.1 %collective-permute-start.9 = (bf16[16,8]{0,1:T(8,128)(2,1)S(1)}, bf16[16,8]{0,1:T(8,128)(2,1)S(1)}, u32[]{:S(2)}, u32[]{:S(2)}) collective-permute-start(bf16[16,8]{0,1:T(8,128)(2,1)S(1)} %convolution_convert_fusion), channel_id=1, source_target_pairs={{0,15},{1,0},{2,1},{3,2},{4,3},{5,4},{6,5},{7,6},{8,7},{9,8},{10,9... | collective-permute-start | bytes 776 | tf_op jit(solution)/shard_map/ppermute | solution.py:15
  43.0 114.5 %copy-start.5 = (f32[256]{0:T(256)}, f32[256]{0:T(256)S(1)}, u32[]{:S(2)}) copy-start(f32[256]{0:T(256)S(1)} %convert_reduce_fusion.4) | copy-start | bytes 3076
  50.8 4.2 %collective-permute-start.2 = (bf16[16,8]{0,1:T(8,128)(2,1)S(1)}, bf16[16,8]{0,1:T(8,128)(2,1)S(1)}, u32[]{:S(2)}, u32[]{:S(2)}) collective-permute-start(bf16[16,8]{0,1:T(8,128)(2,1)S(1)} %collective-permute-done.1), channel_id=1, source_target_pairs={{0,1},{1,2},{2,3},{3,4},{4,5},{5,6},{6,7},{7,8},{8,9},{9,10},{10,1... | collective-permute-start | bytes 776 | tf_op jit(solution)/shard_map/ppermute | solution.py:13
  51.4 4.3 %collective-permute-start.10 = (bf16[16,8]{0,1:T(8,128)(2,1)S(1)}, bf16[16,8]{0,1:T(8,128)(2,1)S(1)}, u32[]{:S(2)}, u32[]{:S(2)}) collective-permute-start(bf16[16,8]{0,1:T(8,128)(2,1)S(1)} %collective-permute-done.9), channel_id=1, source_target_pairs={{0,15},{1,0},{2,1},{3,2},{4,3},{5,4},{6,5},{7,6},{8,7},{9,8},{10,9... | collective-permute-start | bytes 776 | tf_op jit(solution)/shard_map/ppermute | solution.py:15
  55.0 4.2 %collective-permute-start.3 = (bf16[16,8]{0,1:T(8,128)(2,1)S(1)}, bf16[16,8]{0,1:T(8,128)(2,1)S(1)}, u32[]{:S(2)}, u32[]{:S(2)}) collective-permute-start(bf16[16,8]{0,1:T(8,128)(2,1)S(1)} %collective-permute-done.2), channel_id=1, source_target_pairs={{0,1},{1,2},{2,3},{3,4},{4,5},{5,6},{6,7},{7,8},{8,9},{9,10},{10,1... | collective-permute-start | bytes 776 | tf_op jit(solution)/shard_map/ppermute | solution.py:13
  55.7 4.2 %collective-permute-start.11 = (bf16[16,8]{0,1:T(8,128)(2,1)S(1)}, bf16[16,8]{0,1:T(8,128)(2,1)S(1)}, u32[]{:S(2)}, u32[]{:S(2)}) collective-permute-start(bf16[16,8]{0,1:T(8,128)(2,1)S(1)} %collective-permute-done.10), channel_id=1, source_target_pairs={{0,15},{1,0},{2,1},{3,2},{4,3},{5,4},{6,5},{7,6},{8,7},{9,8},{10,9... | collective-permute-start | bytes 776 | tf_op jit(solution)/shard_map/ppermute | solution.py:15
  59.2 4.2 %collective-permute-start.4 = (bf16[16,8]{0,1:T(8,128)(2,1)S(1)}, bf16[16,8]{0,1:T(8,128)(2,1)S(1)}, u32[]{:S(2)}, u32[]{:S(2)}) collective-permute-start(bf16[16,8]{0,1:T(8,128)(2,1)S(1)} %collective-permute-done.3), channel_id=1, source_target_pairs={{0,1},{1,2},{2,3},{3,4},{4,5},{5,6},{6,7},{7,8},{8,9},{9,10},{10,1... | collective-permute-start | bytes 776 | tf_op jit(solution)/shard_map/ppermute | solution.py:13
  59.9 4.2 %collective-permute-start.12 = (bf16[16,8]{0,1:T(8,128)(2,1)S(1)}, bf16[16,8]{0,1:T(8,128)(2,1)S(1)}, u32[]{:S(2)}, u32[]{:S(2)}) collective-permute-start(bf16[16,8]{0,1:T(8,128)(2,1)S(1)} %collective-permute-done.11), channel_id=1, source_target_pairs={{0,15},{1,0},{2,1},{3,2},{4,3},{5,4},{6,5},{7,6},{8,7},{9,8},{10,9... | collective-permute-start | bytes 776 | tf_op jit(solution)/shard_map/ppermute | solution.py:15
  63.5 4.2 %collective-permute-start.5 = (bf16[16,8]{0,1:T(8,128)(2,1)S(1)}, bf16[16,8]{0,1:T(8,128)(2,1)S(1)}, u32[]{:S(2)}, u32[]{:S(2)}) collective-permute-start(bf16[16,8]{0,1:T(8,128)(2,1)S(1)} %collective-permute-done.4), channel_id=1, source_target_pairs={{0,1},{1,2},{2,3},{3,4},{4,5},{5,6},{6,7},{7,8},{8,9},{9,10},{10,1... | collective-permute-start | bytes 776 | tf_op jit(solution)/shard_map/ppermute | solution.py:13
  64.1 4.2 %collective-permute-start.13 = (bf16[16,8]{0,1:T(8,128)(2,1)S(1)}, bf16[16,8]{0,1:T(8,128)(2,1)S(1)}, u32[]{:S(2)}, u32[]{:S(2)}) collective-permute-start(bf16[16,8]{0,1:T(8,128)(2,1)S(1)} %collective-permute-done.12), channel_id=1, source_target_pairs={{0,15},{1,0},{2,1},{3,2},{4,3},{5,4},{6,5},{7,6},{8,7},{9,8},{10,9... | collective-permute-start | bytes 776 | tf_op jit(solution)/shard_map/ppermute | solution.py:15
  67.7 4.2 %collective-permute-start.6 = (bf16[16,8]{0,1:T(8,128)(2,1)S(1)}, bf16[16,8]{0,1:T(8,128)(2,1)S(1)}, u32[]{:S(2)}, u32[]{:S(2)}) collective-permute-start(bf16[16,8]{0,1:T(8,128)(2,1)S(1)} %collective-permute-done.5), channel_id=1, source_target_pairs={{0,1},{1,2},{2,3},{3,4},{4,5},{5,6},{6,7},{7,8},{8,9},{9,10},{10,1... | collective-permute-start | bytes 776 | tf_op jit(solution)/shard_map/ppermute | solution.py:13
  68.4 4.2 %collective-permute-start.14 = (bf16[16,8]{0,1:T(8,128)(2,1)S(1)}, bf16[16,8]{0,1:T(8,128)(2,1)S(1)}, u32[]{:S(2)}, u32[]{:S(2)}) collective-permute-start(bf16[16,8]{0,1:T(8,128)(2,1)S(1)} %collective-permute-done.13), channel_id=1, source_target_pairs={{0,15},{1,0},{2,1},{3,2},{4,3},{5,4},{6,5},{7,6},{8,7},{9,8},{10,9... | collective-permute-start | bytes 776 | tf_op jit(solution)/shard_map/ppermute | solution.py:15
  71.9 4.2 %collective-permute-start.7 = (bf16[16,8]{0,1:T(8,128)(2,1)S(1)}, bf16[16,8]{0,1:T(8,128)(2,1)S(1)}, u32[]{:S(2)}, u32[]{:S(2)}) collective-permute-start(bf16[16,8]{0,1:T(8,128)(2,1)S(1)} %collective-permute-done.6), channel_id=1, source_target_pairs={{0,1},{1,2},{2,3},{3,4},{4,5},{5,6},{6,7},{7,8},{8,9},{9,10},{10,1... | collective-permute-start | bytes 776 | tf_op jit(solution)/shard_map/ppermute | solution.py:13
  72.6 4.2 %collective-permute-start.15 = (bf16[16,8]{0,1:T(8,128)(2,1)S(1)}, bf16[16,8]{0,1:T(8,128)(2,1)S(1)}, u32[]{:S(2)}, u32[]{:S(2)}) collective-permute-start(bf16[16,8]{0,1:T(8,128)(2,1)S(1)} %collective-permute-done.14), channel_id=1, source_target_pairs={{0,15},{1,0},{2,1},{3,2},{4,3},{5,4},{6,5},{7,6},{8,7},{9,8},{10,9... | collective-permute-start | bytes 776 | tf_op jit(solution)/shard_map/ppermute | solution.py:15
  76.1 4.2 %collective-permute-start.8 = (bf16[16,8]{0,1:T(8,128)(2,1)S(1)}, bf16[16,8]{0,1:T(8,128)(2,1)S(1)}, u32[]{:S(2)}, u32[]{:S(2)}) collective-permute-start(bf16[16,8]{0,1:T(8,128)(2,1)S(1)} %collective-permute-done.7), channel_id=1, source_target_pairs={{0,1},{1,2},{2,3},{3,4},{4,5},{5,6},{6,7},{7,8},{8,9},{9,10},{10,1... | collective-permute-start | bytes 776 | tf_op jit(solution)/shard_map/ppermute | solution.py:13
  163.0 6.6 %collective-permute-start = (bf16[16,3072]{1,0:T(8,128)(2,1)S(1)}, bf16[16,3072]{1,0:T(8,128)(2,1)}, u32[]{:S(2)}, u32[]{:S(2)}) collective-permute-start(bf16[16,3072]{1,0:T(8,128)(2,1)S(1)} %fusion.22), channel_id=1, source_target_pairs={{0,16},{16,32},{32,48},{48,64},{64,80},{80,96},{96,112},{112,128},... | collective-permute-start | bytes 294920 | tf_op jit(solution)/shard_map/ppermute | solution.py:23
  208.7 28.2 %copy-start.3 = (f32[3072,1]{0,1:T(1,128)S(1)}, f32[3072,1]{0,1:T(1,128)}, u32[]{:S(2)}) copy-start(f32[3072,1]{0,1:T(1,128)} %slice_convert_fusion) | copy-start | bytes 36868
  208.7 33.2 %copy-start.7 = (f32[256,1]{0,1:T(1,128)S(1)}, f32[256,1]{0,1:T(1,128)}, u32[]{:S(2)}) copy-start(f32[256,1]{0,1:T(1,128)} %get-tuple-element.14) | copy-start | bytes 3076
  239.2 8.6 %collective-permute-start.16 = (bf16[16,3072]{1,0:T(8,128)(2,1)S(1)}, bf16[16,3072]{1,0:T(8,128)(2,1)S(1)}, u32[]{:S(2)}, u32[]{:S(2)}) collective-permute-start(bf16[16,3072]{1,0:T(8,128)(2,1)S(1)} %fusion.20), channel_id=1, source_target_pairs={{16,0},{32,16},{48,32},{64,48},{80,64},{96,80},{112,96},{128,112},... | collective-permute-start | bytes 294920 | tf_op jit(solution)/shard_map/ppermute | solution.py:23
  (6 other events, 86.2 us)
Sparse Core Ops, SparseCore 0:
  38.9 118.5 all-reduce.1
  159.7 42.1 all-gather.3
